TPU v7x, 32 devices: a whole 2x2x4 slice. The times are simulated.
32 devices in a mesh: space: 4 (over y, x), scen: 8 (over z, core).
Axes of the slice: x: 2, y: 2, z: 4, core: 2. Of those that a mesh axis runs over, the one named last changes fastest.
Arguments:
- tracers: float32 [8, 2, 20, 32, 512], P('scen', None, None, None, 'space'), may hold values from -6 to 6
- diffusivity: float32 [2, 20, 32, 512], P(None, None, 'scen', 'space'), may hold values from 0.02 to 0.16
- level_count: int32 [32, 512], P(None, 'space'), may hold values from 0 to 20
- shelf_mask: int32 [32, 512], P(None, 'space'), may hold values 0 or 1
- cotangent: float32 [8, 2, 20, 32, 512], P('scen', None, None, None, 'space'), may hold values from -6 to 6
Outputs:
- final_tracers: float32 [8, 2, 20, 32, 512], P('scen', None, None, None, 'space')
- adjoint_tracers: float32 [8, 2, 20, 32, 512], P('scen', None, None, None, 'space')
- kappa_grad: float32 [2, 20, 32, 512], P(None, None, 'scen', 'space')
Inputs may be any that keep to these rules, and one draw needn't show every extreme that they name: `level_count`: wet levels of a column, counted from the surface; 0 marks land.
All inputs are finite; a program needn't handle non-finite values. No bound on the sum of `shelf_mask` on one device may be relied on, other than what follows from the above.
Results may differ from a plain program's by a relative error of at most 0.00002.
Values sent between devices are 32-bit elements; how exact they have to be, the bound alone decides.
No kernel may reach another device: no remote copies, remote signals or barrier semaphores. Data moves between devices by JAX's collectives and lax.ppermute only.
A program may use at most 64 MiB of HBM per device.

v0:
```python
import jax
import jax.numpy as jnp
from jax import lax
from jax.sharding import PartitionSpec as P

STEPS = 2
vertical_rate = 0.1
thaw_rate = 0.3


def with_halo(block, sides, width):
    for axis, dim in sides:
        count = lax.axis_size(axis)
        forward = [(i, i + 1) for i in range(count - 1)]
        forward.append((count - 1, 0))
        backward = [(target, source) for source, target in forward]
        low = lax.ppermute(
            lax.slice_in_dim(block, block.shape[dim] - width, None, axis=dim), axis, forward
        )
        high = lax.ppermute(lax.slice_in_dim(block, 0, width, axis=dim), axis, backward)
        block = jnp.concatenate([low, block, high], axis=dim)
    return block


def from_partner(value, axis, stride):
    return lax.ppermute(value, axis, [(i, i ^ 1 << stride) for i in range(lax.axis_size(axis))])


def with_edges(field_now):
    return with_halo(field_now, (("space", 3),), 1)


def partner_row(top_row):
    exchanged = top_row
    for bit_index in range(lax.axis_size("space").bit_length() - 1):
        exchanged = from_partner(exchanged, "space", bit_index)
    return exchanged[:, :, ::-1]


def sources_of(wetness, shelf_mask):
    below_wet = jnp.concatenate([wetness[1:], jnp.zeros_like(wetness[:1])], axis=0)
    heat_source = thaw_rate * shelf_mask.astype(jnp.float32)[None] * wetness * (1.0 - below_wet)
    return jnp.stack([heat_source, jnp.zeros_like(heat_source)])


def operate_on(tracer_now, coeffs):
    east_coeff, north_coeff, fold_coeff, down_coeff = coeffs
    edged_field = with_edges(tracer_now)
    east_flux = east_coeff * (edged_field[..., 1:] - edged_field[..., :-1])
    across_x = east_flux[..., 1:] - east_flux[..., :-1]
    north_flux = north_coeff * (tracer_now[:, :, 1:] - tracer_now[:, :, :-1])
    top_row = tracer_now[:, :, -1]
    partner = partner_row(top_row)
    fold_flux = fold_coeff * (partner - top_row)
    all_north = jnp.concatenate([north_flux, fold_flux[:, :, None]], axis=2)
    zero_row = jnp.zeros_like(all_north[:, :, :1])
    across_y = all_north - jnp.concatenate([zero_row, all_north[:, :, :-1]], axis=2)
    down_flux = down_coeff * (tracer_now[:, 1:] - tracer_now[:, :-1])
    zero_level = jnp.zeros_like(down_flux[:, :1])
    across_z = jnp.concatenate([down_flux, zero_level], axis=1) - jnp.concatenate(
        [zero_level, down_flux], axis=1
    )
    return (across_x + across_y + across_z, edged_field, partner)


def on_device(tracers, diffusivity, level_count, shelf_mask, cotangent):
    full_kappa = lax.all_gather(diffusivity, "scen", axis=2, tiled=True)
    levels = lax.broadcasted_iota(jnp.int32, (full_kappa.shape[1],) + level_count.shape, 0)
    wetness = (levels < level_count[None]).astype(jnp.float32)
    sources = sources_of(wetness, shelf_mask)
    edged_coeff = with_edges(jnp.stack([wetness, full_kappa[0]]))
    wet_edge = edged_coeff[0]
    kappa_edge = edged_coeff[1]
    east_mask = wet_edge[..., :-1] * wet_edge[..., 1:]
    east_coeff = kappa_edge[..., :-1] * east_mask
    north_kappa = full_kappa[1]
    north_mask = wetness[:, :-1] * wetness[:, 1:]
    north_coeff = north_kappa[:, :-1] * north_mask
    top_wet = wetness[:, -1]
    top_kappa = north_kappa[:, -1]
    partner_coeff = partner_row(jnp.stack([top_wet, top_kappa]))
    fold_mask = top_wet * partner_coeff[0]
    fold_coeff = 0.5 * (top_kappa + partner_coeff[1]) * fold_mask
    down_coeff = vertical_rate * wetness[:-1] * wetness[1:]
    coeffs = (east_coeff, north_coeff, fold_coeff, down_coeff)
    tracer_now = tracers[0]
    stored = []
    for substep in range(STEPS):
        change, edged_field, partner = operate_on(tracer_now, coeffs)
        stored.append((tracer_now, edged_field, partner))
        tracer_now = wetness * (tracer_now + change + sources)
    adjoint = cotangent[0]
    summed = None
    for substep in reversed(range(STEPS)):
        weighted = wetness * adjoint
        change, weighted_edge, weighted_partner = operate_on(weighted, coeffs)
        adjoint = weighted + change
        before, before_edge, before_partner = stored[substep]
        grad_east = jnp.sum(
            east_mask[..., 1:]
            * (before_edge[..., 2:] - before_edge[..., 1:-1])
            * (weighted_edge[..., 1:-1] - weighted_edge[..., 2:]),
            axis=0,
        )
        grad_inner = jnp.sum(
            north_mask
            * (before[:, :, 1:] - before[:, :, :-1])
            * (weighted[:, :, :-1] - weighted[:, :, 1:]),
            axis=0,
        )
        grad_fold = jnp.sum(
            0.5
            * fold_mask
            * (before_partner - before[:, :, -1])
            * (weighted[:, :, -1] - weighted_partner),
            axis=0,
        )
        grad_term = jnp.stack(
            [grad_east, jnp.concatenate([grad_inner, grad_fold[:, None]], axis=1)]
        )
        summed = grad_term if summed is None else summed + grad_term
    kappa_grad = lax.psum_scatter(summed, "scen", scatter_dimension=2, tiled=True)
    return (tracer_now[None], adjoint[None], kappa_grad)


def solution(mesh):
    placed = (
        P("scen", None, None, None, "space"),
        P(None, None, "scen", "space"),
        P(None, "space"),
        P(None, "space"),
        P("scen", None, None, None, "space"),
    )
    return jax.shard_map(
        on_device,
        mesh=mesh,
        in_specs=placed,
        out_specs=(
            P("scen", None, None, None, "space"),
            P("scen", None, None, None, "space"),
            P(None, None, "scen", "space"),
        ),
        check_vma=False,
    )
```

profile of v0, /device:TPU:0, one launch (start us, length us, event | category | flops | bytes accessed | tf_op | source)
XLA Modules:
  0.0 178.3 jit_solution(11726017105144906224)
XLA Ops:
  7.2 0.9 copy.135
  8.1 0.7 fusion.41
  8.9 17.0 %all_gather.3 = f32[2,20,32,128]{3,0,1,2:T(2,128)S(1)} all-gather(f32[2,20,4,128]{3,0,1,2:T(2,128)S(1)} %copy.135), channel_id=1, replica_groups=mesh['space'=4,'scen'=8] {'scen'}, dimensions={2}, use_global_device_ids=true | all-gather | bytes 737280 | tf_op jit(solution)/shard_map/all_gather | solution.py:67
  25.9 1.2 fusion.47
  27.2 1.6 collective-permute-start.4
  29.3 0.7 fusion.48
  30.0 0.9 copy.142
  30.9 1.5 collective-permute-start.2
  33.3 1.0 copy.172
  34.6 0.9 copy.138
  35.5 2.4 %collective-permute-start.1 = (f32[2,20,32,1]{2,0,3,1:T(2,128)}, f32[2,20,32,1]{2,0,3,1:T(2,128)}, u32[]{:S(2)}, u32[]{:S(2)}) collective-permute-start(f32[2,20,32,1]{2,0,3,1:T(2,128)} %copy.138), channel_id=1, source_target_pairs={{8,0},{16,8},{24,16},{0,24},{9,1},{17,9},{25,17},{1,25},{10,2},{18... | collective-permute-start | bytes 15368 | tf_op jit(solution)/shard_map/ppermute | solution.py:20
  37.9 0.9 copy.137
  39.1 0.6 copy-done
  40.2 0.7 bitcast_multiply_fusion
  40.9 1.7 fusion.45
  43.1 1.6 fusion.38
  44.8 1.6 subtract_multiply_fusion.1
  46.5 1.1 copy.149
  47.5 0.9 copy.164
  48.5 2.0 %copy.157 = f32[2,20,32,1]{2,0,3,1:T(2,128)} copy(f32[2,20,32,1]{3,0,1,2:T(2,128)} %get-tuple-element.37) | data formatting | bytes 10240 | tf_op jit(solution)/shard_map/slice | solution.py:18
  50.5 0.9 copy.155
  51.4 2.9 %collective-permute-start.12 = (f32[2,20,32,1]{2,0,3,1:T(2,128)}, f32[2,20,32,1]{2,0,3,1:T(2,128)}, u32[]{:S(2)}, u32[]{:S(2)}) collective-permute-start(f32[2,20,32,1]{2,0,3,1:T(2,128)} %copy.155), channel_id=1, source_target_pairs={{8,0},{16,8},{24,16},{0,24},{9,1},{17,9},{25,17},{1,25},{10,2},{18... | collective-permute-start | bytes 15368 | tf_op jit(solution)/shard_map/ppermute | solution.py:20
  54.3 1.0 copy.139
  55.6 1.9 %copy.140 = f32[2,20,32,1]{3,2,1,0:T(8,128)} copy(f32[2,20,32,1]{2,0,3,1:T(2,128)} %collective-permute-done.1) | data formatting | bytes 10240 | tf_op jit(solution)/shard_map/ppermute | solution.py:20
  57.5 1.7 pad_maximum_fusion.4
  59.2 1.1 slice_multiply_fusion.1
  60.7 2.0 %collective-permute-start.14 = (f32[2,20,128]{2,0,1:T(2,128)S(1)}, f32[2,20,128]{2,0,1:T(2,128)}, u32[]{:S(2)}, u32[]{:S(2)}) collective-permute-start(f32[2,20,128]{2,0,1:T(2,128)S(1)} %slice_bitcast_fusion.3), channel_id=1, source_target_pairs={{0,8},{8,0},{16,24},{24,16},{1,9},{9,1},{17,25},{25,17},{2,10},{10... | collective-permute-start | bytes 61448 | tf_op jit(solution)/shard_map/ppermute | solution.py:26
  63.4 1.2 copy.145
  64.5 1.9 %copy.156 = f32[2,20,32,1]{3,0,1,2:T(2,128)} copy(f32[2,20,32,1]{2,0,3,1:T(2,128)} %collective-permute-done.12) | data formatting | bytes 10240 | tf_op jit(solution)/shard_map/ppermute | solution.py:20
  66.4 1.9 %copy.158 = f32[2,20,32,1]{3,0,1,2:T(2,128)} copy(f32[2,20,32,1]{2,0,3,1:T(2,128)} %collective-permute-done.13) | data formatting | bytes 10240 | tf_op jit(solution)/shard_map/ppermute | solution.py:17
  68.3 1.5 collective-permute-start.5
  69.8 5.6 %fusion.3 = (f32[2,20,32,129]{3,0,1,2:T(2,128)}, f32[2,20,32,129]{3,0,1,2:T(2,128)}) fusion(f32[2,20,32,1]{3,0,1,2:T(2,128)} %copy.156, f32[2,20,32,128]{3,0,1,2:T(2,128)S(1)} %bitcast_multiply_fusion, f32[2,20,32,1]{3,0,1,2:T(2,128)} %copy.158, f32[20,32,129]{2,0,1:T(8,128)S(1)} %copy.141, f32[2,20,32,128]{3,0,1,2:T(2,128)S(1)} %bitcast.82, ...), kind=kLoop, calls=%fused_computation.15 | loop fusion | flops 1320960 | bytes 2982400 | tf_op jit(solution)/shard_map/mul | solution.py:49
  75.5 1.0 copy.163
  76.5 0.6 collective-permute-start.15
  77.0 1.5 collective-permute-start.7
  78.8 1.6 collective-permute-done.15
  81.0 6.4 %fusion.33 = (f32[2,20,32,128]{3,0,1,2:T(2,128)S(1)}, f32[2,20,32,128]{3,0,1,2:T(2,128)S(1)}) fusion(f32[2,19,32,128]{3,0,1,2:T(2,128)} %get-tuple-element.51, f32[2,20,31,128]{3,0,1,2:T(2,128)} %get-tuple-element.53, f32[2,20,1,128]{3,0,1,2:T(2,128)S(1)} %get-tuple-element.61, f32[2,20,32,129]{3,0,1,2:T(2,128)} %get-tuple-element.29, ...), kind=kLoop, calls=%fused_computation.65 | loop fusion | flops 2949120 | bytes 8454144 | tf_op jit(solution)/shard_map/mul | solution.py:95
  87.4 1.7 fusion.44
  89.1 1.8 fusion.46
  90.9 2.0 %collective-permute-start.10 = (f32[2,20,128]{2,0,1:T(2,128)S(1)}, f32[2,20,128]{2,0,1:T(2,128)}, u32[]{:S(2)}, u32[]{:S(2)}) collective-permute-start(f32[2,20,128]{2,0,1:T(2,128)S(1)} %slice_bitcast_fusion.4), channel_id=1, source_target_pairs={{0,8},{8,0},{16,24},{24,16},{1,9},{9,1},{17,25},{25,17},{2,10},{10... | collective-permute-start | bytes 61448 | tf_op jit(solution)/shard_map/ppermute | solution.py:26
  92.9 6.6 %multiply_reduce_fusion = (f32[20,31,128]{2,0,1:T(8,128)}, f32[20,31,128]{2,0,1:T(8,128)}, f32[2,20,31,128]{3,0,1,2:T(2,128)}, f32[2,20,31,128]{3,0,1,2:T(2,128)}) fusion(f32[2,20,32,128]{3,0,1,2:T(2,128)S(1)} %get-tuple-element.49, f32[20,31,128]{2,0,1:T(8,128)S(1)} %copy-done.18, f32[2,20,32,128]{3,0,1,2:T(2,128)S(1)} %bitcast.84, ...), kind=kLoop, calls=%fused_computation.71 | loop fusion | flops 1904640 | bytes 7618560 | tf_op jit(solution)/shard_map/reduce_sum | solution.py:105
  99.5 2.0 %copy.159 = f32[2,20,32,1]{2,0,3,1:T(2,128)} copy(f32[2,20,32,1]{3,0,1,2:T(2,128)} %get-tuple-element.36) | data formatting | bytes 10240 | tf_op jit(solution)/shard_map/slice | solution.py:20
  101.5 2.9 %collective-permute-start.16 = (f32[2,20,32,1]{2,0,3,1:T(2,128)}, f32[2,20,32,1]{2,0,3,1:T(2,128)}, u32[]{:S(2)}, u32[]{:S(2)}) collective-permute-start(f32[2,20,32,1]{2,0,3,1:T(2,128)} %copy.159), channel_id=1, source_target_pairs={{8,0},{16,8},{24,16},{0,24},{9,1},{17,9},{25,17},{1,25},{10,2},{18... | collective-permute-start | bytes 15368 | tf_op jit(solution)/shard_map/ppermute | solution.py:20
  104.4 2.0 %copy.150 = f32[2,20,32,1]{2,0,3,1:T(2,128)} copy(f32[2,20,32,1]{3,0,1,2:T(2,128)} %get-tuple-element.40) | data formatting | bytes 10240 | tf_op jit(solution)/shard_map/slice | solution.py:20
  106.4 2.7 %fusion.37 = (f32[2,19,32,128]{3,0,1,2:T(2,128)}, f32[2,19,32,128]{3,0,1,2:T(2,128)}) fusion(f32[2,20,32,128]{3,0,1,2:T(2,128)S(1)} %get-tuple-element.49, f32[19,32,128]{2,0,1:T(8,128)} %copy-done.5, f32[2,20,32,128]{3,0,1,2:T(2,128)S(1)} %get-tuple-element.50), kind=kLoop, calls=%fused_computation.76 | loop fusion | flops 622592 | bytes 4046848 | tf_op jit(solution)/shard_map/mul | solution.py:58
  109.2 1.4 copy.161
  110.6 2.0 %collective-permute-start.17 = (f32[2,20,32,1]{2,0,3,1:T(2,128)S(1)}, f32[2,20,32,1]{2,0,3,1:T(2,128)}, u32[]{:S(2)}, u32[]{:S(2)}) collective-permute-start(f32[2,20,32,1]{2,0,3,1:T(2,128)S(1)} %copy.161), channel_id=1, source_target_pairs={{0,8},{8,16},{16,24},{24,0},{1,9},{9,17},{17,25},{25,1},{2,10},{10... | collective-permute-start | bytes 15368 | tf_op jit(solution)/shard_map/ppermute | solution.py:17
  112.6 2.0 %copy.152 = f32[2,20,32,1]{2,0,3,1:T(2,128)} copy(f32[2,20,32,1]{3,0,1,2:T(2,128)} %get-tuple-element.39) | data formatting | bytes 10240 | tf_op jit(solution)/shard_map/slice | solution.py:18
  114.6 1.9 %copy.160 = f32[2,20,32,1]{3,0,1,2:T(2,128)} copy(f32[2,20,32,1]{2,0,3,1:T(2,128)} %collective-permute-done.16) | data formatting | bytes 10240 | tf_op jit(solution)/shard_map/ppermute | solution.py:20
  116.5 1.9 %copy.151 = f32[2,20,32,1]{3,0,1,2:T(2,128)} copy(f32[2,20,32,1]{2,0,3,1:T(2,128)} %collective-permute-done.8) | data formatting | bytes 10240 | tf_op jit(solution)/shard_map/ppermute | solution.py:20
  118.4 1.5 collective-permute-start.11
  120.4 8.7 %fusion.36 = (f32[20,32,128]{2,0,1:T(8,128)}, f32[20,32,128]{2,0,1:T(8,128)}) fusion(f32[2,20,32,128]{3,0,1,2:T(2,128)S(1)} %get-tuple-element.49, f32[2,20,32,1]{3,0,1,2:T(2,128)} %copy.160, f32[2,20,32,128]{3,0,1,2:T(2,128)S(1)} %bitcast.85, f32[2,20,32,1]{3,0,1,2:T(2,128)} %copy-done.2, f32[20,32,128]{2,0,1:T(8,128)} %copy.163, ...), kind=kLoop, calls=%fused_computation.68 | loop fusion | flops 2129920 | bytes 3624960 | tf_op jit(solution)/shard_map/reduce_sum | solution.py:99
  129.1 1.9 %copy.162 = f32[2,20,32,1]{3,0,1,2:T(2,128)} copy(f32[2,20,32,1]{2,0,3,1:T(2,128)} %collective-permute-done.17) | data formatting | bytes 10240 | tf_op jit(solution)/shard_map/ppermute | solution.py:17
  131.0 1.9 %copy.153 = f32[2,20,32,1]{3,0,1,2:T(2,128)} copy(f32[2,20,32,1]{2,0,3,1:T(2,128)} %collective-permute-done.9) | data formatting | bytes 10240 | tf_op jit(solution)/shard_map/ppermute | solution.py:17
  133.3 1.1 maximum_bitcast_fusion.1
  134.3 1.0 maximum_bitcast_fusion
  135.5 1.0 copy.165
  137.1 4.8 %fusion.1 = (f32[2,20,32,129]{3,0,1,2:T(2,128)S(1)}, f32[2,20,32,129]{3,0,1,2:T(2,128)S(1)}) fusion(f32[2,20,32,1]{3,0,1,2:T(2,128)S(1)} %copy-done.3, f32[2,20,32,128]{3,0,1,2:T(2,128)S(1)} %get-tuple-element.49, f32[2,20,32,1]{3,0,1,2:T(2,128)} %copy.162, f32[20,32,129]{2,0,1:T(8,128)S(1)} %copy.141, f32[2,20,32,128]{3,0,1,2:T(2,128)S(1)} %get-tuple-element.50, ...), kind=kLoop, calls=%fused_computation.13 | loop fusion | flops 1320960 | bytes 2982400 | tf_op jit(solution)/shard_map/mul | solution.py:49
  141.9 1.4 fusion.34
  143.4 1.0 copy.167
  144.7 1.6 fusion.10
  146.3 1.0 copy.166
  147.3 22.6 %reduce-scatter.2.cloned.1.call-done = f32[2,20,4,128]{3,1,0,2:T(8,128)} async-done(((f32[2,20,32,128]{3,1,0,2:T(8,128)}), f32[2,20,4,128]{3,1,0,2:T(8,128)}) %reduce-scatter.2.cloned.1.call-update) | async-done | bytes 81936 | tf_op jit(solution)/shard_map/reduce_scatter | solution.py:122
  169.9 1.6 copy.168
  (107 shorter events, 7.5 us)
Async XLA Ops:
  7.2 162.7 %reduce-scatter.2.cloned.1.call-start = ((), (), s32[]{:S(2)}) async-start(), calls=%async_computation.1 | async-start | bytes 884736 | tf_op jit(solution)/shard_map/reduce_scatter | solution.py:122
  8.9 19.9 %copy-start.10 = (f32[1,2,20,32,128]{4,3,2,1,0:T(8,128)S(1)}, f32[1,2,20,32,128]{4,3,2,1,0:T(8,128)}, u32[]{:S(2)}) copy-start(f32[1,2,20,32,128]{4,3,2,1,0:T(8,128)} %param.5) | copy-start | bytes 1966084
  27.2 41.1 %collective-permute-start.4 = (f32[2,20,128]{2,0,1:T(2,128)S(1)}, f32[2,20,128]{2,0,1:T(2,128)}, u32[]{:S(2)}, u32[]{:S(2)}) collective-permute-start(f32[2,20,128]{2,0,1:T(2,128)S(1)} %pad_maximum_fusion.6), channel_id=1, source_target_pairs={{0,8},{8,0},{16,24},{24,16},{1,9},{9,1},{17,25},{25,17},{2,10},{10... | collective-permute-start | bytes 61448 | tf_op jit(solution)/shard_map/ppermute | solution.py:26
  30.0 3.3 %copy-start.20 = (s32[32,128]{1,0:T(8,128)S(1)}, s32[32,128]{1,0:T(8,128)}, u32[]{:S(2)}) copy-start(s32[32,128]{1,0:T(8,128)} %param.7) | copy-start | bytes 49156
  30.9 29.8 %collective-permute-start.2 = (f32[2,20,32,1]{2,0,3,1:T(2,128)}, f32[2,20,32,1]{2,0,3,1:T(2,128)S(1)}, u32[]{:S(2)}, u32[]{:S(2)}) collective-permute-start(f32[2,20,32,1]{2,0,3,1:T(2,128)} %copy.142), channel_id=1, source_target_pairs={{8,0},{16,8},{24,16},{0,24},{9,1},{17,9},{25,17},{1,25},{10,2},{18... | collective-permute-start | bytes 15368 | tf_op jit(solution)/shard_map/ppermute | solution.py:20
  32.7 30.5 %collective-permute-start.3 = (f32[2,20,32,1]{2,0,3,1:T(2,128)S(1)}, f32[2,20,32,1]{2,0,3,1:T(2,128)S(1)}, u32[]{:S(2)}, u32[]{:S(2)}) collective-permute-start(f32[2,20,32,1]{2,0,3,1:T(2,128)S(1)} %copy.144), channel_id=1, source_target_pairs={{0,8},{8,16},{16,24},{24,0},{1,9},{9,17},{17,25},{25,1},{2,10},{10... | collective-permute-start | bytes 15368 | tf_op jit(solution)/shard_map/ppermute | solution.py:17
  35.5 19.8 %collective-permute-start.1 = (f32[2,20,32,1]{2,0,3,1:T(2,128)}, f32[2,20,32,1]{2,0,3,1:T(2,128)}, u32[]{:S(2)}, u32[]{:S(2)}) collective-permute-start(f32[2,20,32,1]{2,0,3,1:T(2,128)} %copy.138), channel_id=1, source_target_pairs={{8,0},{16,8},{24,16},{0,24},{9,1},{17,9},{25,17},{1,25},{10,2},{18... | collective-permute-start | bytes 15368 | tf_op jit(solution)/shard_map/ppermute | solution.py:20
  38.8 12.6 %collective-permute-start = (f32[2,20,32,1]{2,0,3,1:T(2,128)}, f32[2,20,32,1]{2,0,3,1:T(2,128)}, u32[]{:S(2)}, u32[]{:S(2)}) collective-permute-start(f32[2,20,32,1]{2,0,3,1:T(2,128)} %copy.137), channel_id=1, source_target_pairs={{0,8},{8,16},{16,24},{24,0},{1,9},{9,17},{17,25},{25,1},{2,10},{10... | collective-permute-start | bytes 15368 | tf_op jit(solution)/shard_map/ppermute | solution.py:17
  39.0 0.7 copy-start
  39.0 1.2 copy-start.9
  40.9 1.8 copy-start.21
  42.9 1.9 %copy-start.6 = (f32[20,31,128]{2,0,1:T(8,128)}, f32[20,31,128]{2,0,1:T(8,128)S(1)}, u32[]{:S(2)}) copy-start(f32[20,31,128]{2,0,1:T(8,128)S(1)} %copy.147) | copy-start | bytes 952324
  43.1 1.7 copy-start.5
  46.4 4.1 %copy-start.11 = (f32[2,20,32,1]{3,0,1,2:T(2,128)S(1)}, f32[2,20,32,1]{3,0,1,2:T(2,128)}, u32[]{:S(2)}) copy-start(f32[2,20,32,1]{3,0,1,2:T(2,128)} %get-tuple-element.38) | copy-start | bytes 15364
  51.4 13.2 %collective-permute-start.12 = (f32[2,20,32,1]{2,0,3,1:T(2,128)}, f32[2,20,32,1]{2,0,3,1:T(2,128)}, u32[]{:S(2)}, u32[]{:S(2)}) collective-permute-start(f32[2,20,32,1]{2,0,3,1:T(2,128)} %copy.155), channel_id=1, source_target_pairs={{8,0},{16,8},{24,16},{0,24},{9,1},{17,9},{25,17},{1,25},{10,2},{18... | collective-permute-start | bytes 15368 | tf_op jit(solution)/shard_map/ppermute | solution.py:20
  55.4 11.1 %collective-permute-start.13 = (f32[2,20,32,1]{2,0,3,1:T(2,128)}, f32[2,20,32,1]{2,0,3,1:T(2,128)}, u32[]{:S(2)}, u32[]{:S(2)}) collective-permute-start(f32[2,20,32,1]{2,0,3,1:T(2,128)} %copy.157), channel_id=1, source_target_pairs={{0,8},{8,16},{16,24},{24,0},{1,9},{9,17},{17,25},{25,1},{2,10},{10... | collective-permute-start | bytes 15368 | tf_op jit(solution)/shard_map/ppermute | solution.py:17
  60.7 15.7 %collective-permute-start.14 = (f32[2,20,128]{2,0,1:T(2,128)S(1)}, f32[2,20,128]{2,0,1:T(2,128)}, u32[]{:S(2)}, u32[]{:S(2)}) collective-permute-start(f32[2,20,128]{2,0,1:T(2,128)S(1)} %slice_bitcast_fusion.3), channel_id=1, source_target_pairs={{0,8},{8,0},{16,24},{24,16},{1,9},{9,1},{17,25},{25,17},{2,10},{10... | collective-permute-start | bytes 61448 | tf_op jit(solution)/shard_map/ppermute | solution.py:26
  63.2 12.1 %copy-start.2 = (f32[2,20,32,1]{3,0,1,2:T(2,128)}, f32[2,20,32,1]{3,0,1,2:T(2,128)S(1)}, u32[]{:S(2)}) copy-start(f32[2,20,32,1]{3,0,1,2:T(2,128)S(1)} %copy.143) | copy-start | bytes 15364
  63.2 13.8 %collective-permute-start.6 = (f32[2,20,128]{2,0,1:T(2,128)S(1)}, f32[2,20,128]{2,0,1:T(2,128)S(1)}, u32[]{:S(2)}, u32[]{:S(2)}) collective-permute-start(f32[2,20,128]{2,0,1:T(2,128)S(1)} %slice_bitcast_fusion.5), channel_id=1, source_target_pairs={{0,8},{8,0},{16,24},{24,16},{1,9},{9,1},{17,25},{25,17},{2,10},{10... | collective-permute-start | bytes 61448 | tf_op jit(solution)/shard_map/ppermute | solution.py:26
  68.3 7.0 %copy-start.19 = (f32[20,32,129]{2,1,0:T(8,128)S(1)}, f32[20,32,129]{2,1,0:T(8,128)}, u32[]{:S(2)}) copy-start(f32[20,32,129]{2,1,0:T(8,128)} %get-tuple-element.24) | copy-start | bytes 990724
  68.3 10.2 %collective-permute-start.5 = (f32[2,20,128]{2,0,1:T(2,128)}, f32[2,20,128]{2,0,1:T(2,128)S(1)}, u32[]{:S(2)}, u32[]{:S(2)}) collective-permute-start(f32[2,20,128]{2,0,1:T(2,128)} %collective-permute-done.4), channel_id=1, source_target_pairs={{0,16},{8,24},{16,0},{24,8},{1,17},{9,25},{17,1},{25,9},{2,18},{10... | collective-permute-start | bytes 61448 | tf_op jit(solution)/shard_map/ppermute | solution.py:26
  76.5 4.0 %collective-permute-start.15 = (f32[2,20,128]{2,0,1:T(2,128)}, f32[2,20,128]{2,0,1:T(2,128)S(1)}, u32[]{:S(2)}, u32[]{:S(2)}) collective-permute-start(f32[2,20,128]{2,0,1:T(2,128)} %collective-permute-done.14), channel_id=1, source_target_pairs={{0,16},{8,24},{16,0},{24,8},{1,17},{9,25},{17,1},{25,9},{2,18},{10... | collective-permute-start | bytes 61448 | tf_op jit(solution)/shard_map/ppermute | solution.py:26
  77.0 3.8 %collective-permute-start.7 = (f32[2,20,128]{2,0,1:T(2,128)S(1)}, f32[2,20,128]{2,0,1:T(2,128)S(1)}, u32[]{:S(2)}, u32[]{:S(2)}) collective-permute-start(f32[2,20,128]{2,0,1:T(2,128)S(1)} %collective-permute-done.6), channel_id=1, source_target_pairs={{0,16},{8,24},{16,0},{24,8},{1,17},{9,25},{17,1},{25,9},{2,18},{10... | collective-permute-start | bytes 61448 | tf_op jit(solution)/shard_map/ppermute | solution.py:26
  89.1 3.8 %copy-start.7 = (f32[20,31,128]{2,0,1:T(8,128)S(1)}, f32[20,31,128]{2,0,1:T(8,128)}, u32[]{:S(2)}) copy-start(f32[20,31,128]{2,0,1:T(8,128)} %copy-done.6) | copy-start | bytes 952324
  89.1 3.8 %copy-start.18 = (f32[20,31,128]{2,0,1:T(8,128)S(1)}, f32[20,31,128]{2,0,1:T(8,128)}, u32[]{:S(2)}) copy-start(f32[20,31,128]{2,0,1:T(8,128)} %copy.164) | copy-start | bytes 952324
  90.9 27.5 %collective-permute-start.10 = (f32[2,20,128]{2,0,1:T(2,128)S(1)}, f32[2,20,128]{2,0,1:T(2,128)}, u32[]{:S(2)}, u32[]{:S(2)}) collective-permute-start(f32[2,20,128]{2,0,1:T(2,128)S(1)} %slice_bitcast_fusion.4), channel_id=1, source_target_pairs={{0,8},{8,0},{16,24},{24,16},{1,9},{9,1},{17,25},{25,17},{2,10},{10... | collective-permute-start | bytes 61448 | tf_op jit(solution)/shard_map/ppermute | solution.py:26
  92.9 27.0 %collective-permute-start.18 = (f32[2,20,128]{2,0,1:T(2,128)S(1)}, f32[2,20,128]{2,0,1:T(2,128)}, u32[]{:S(2)}, u32[]{:S(2)}) collective-permute-start(f32[2,20,128]{2,0,1:T(2,128)S(1)} %slice_bitcast_fusion.2), channel_id=1, source_target_pairs={{0,8},{8,0},{16,24},{24,16},{1,9},{9,1},{17,25},{25,17},{2,10},{10... | collective-permute-start | bytes 61448 | tf_op jit(solution)/shard_map/ppermute | solution.py:26
  101.5 13.1 %collective-permute-start.16 = (f32[2,20,32,1]{2,0,3,1:T(2,128)}, f32[2,20,32,1]{2,0,3,1:T(2,128)}, u32[]{:S(2)}, u32[]{:S(2)}) collective-permute-start(f32[2,20,32,1]{2,0,3,1:T(2,128)} %copy.159), channel_id=1, source_target_pairs={{8,0},{16,8},{24,16},{0,24},{9,1},{17,9},{25,17},{1,25},{10,2},{18... | collective-permute-start | bytes 15368 | tf_op jit(solution)/shard_map/ppermute | solution.py:20
  106.4 10.1 %collective-permute-start.8 = (f32[2,20,32,1]{2,0,3,1:T(2,128)}, f32[2,20,32,1]{2,0,3,1:T(2,128)}, u32[]{:S(2)}, u32[]{:S(2)}) collective-permute-start(f32[2,20,32,1]{2,0,3,1:T(2,128)} %copy.150), channel_id=1, source_target_pairs={{8,0},{16,8},{24,16},{0,24},{9,1},{17,9},{25,17},{1,25},{10,2},{18... | collective-permute-start | bytes 15368 | tf_op jit(solution)/shard_map/ppermute | solution.py:20
  110.6 18.5 %collective-permute-start.17 = (f32[2,20,32,1]{2,0,3,1:T(2,128)S(1)}, f32[2,20,32,1]{2,0,3,1:T(2,128)}, u32[]{:S(2)}, u32[]{:S(2)}) collective-permute-start(f32[2,20,32,1]{2,0,3,1:T(2,128)S(1)} %copy.161), channel_id=1, source_target_pairs={{0,8},{8,16},{16,24},{24,0},{1,9},{9,17},{17,25},{25,1},{2,10},{10... | collective-permute-start | bytes 15368 | tf_op jit(solution)/shard_map/ppermute | solution.py:17
  114.6 16.4 %collective-permute-start.9 = (f32[2,20,32,1]{2,0,3,1:T(2,128)}, f32[2,20,32,1]{2,0,3,1:T(2,128)}, u32[]{:S(2)}, u32[]{:S(2)}) collective-permute-start(f32[2,20,32,1]{2,0,3,1:T(2,128)} %copy.152), channel_id=1, source_target_pairs={{0,8},{8,16},{16,24},{24,0},{1,9},{9,17},{17,25},{25,1},{2,10},{10... | collective-permute-start | bytes 15368 | tf_op jit(solution)/shard_map/ppermute | solution.py:17
  118.4 14.5 %collective-permute-start.11 = (f32[2,20,128]{2,0,1:T(2,128)}, f32[2,20,128]{2,0,1:T(2,128)S(1)}, u32[]{:S(2)}, u32[]{:S(2)}) collective-permute-start(f32[2,20,128]{2,0,1:T(2,128)} %collective-permute-done.10), channel_id=1, source_target_pairs={{0,16},{8,24},{16,0},{24,8},{1,17},{9,25},{17,1},{25,9},{2,18},{10... | collective-permute-start | bytes 61448 | tf_op jit(solution)/shard_map/ppermute | solution.py:26
  119.8 13.1 %collective-permute-start.19 = (f32[2,20,128]{2,0,1:T(2,128)}, f32[2,20,128]{2,0,1:T(2,128)S(1)}, u32[]{:S(2)}, u32[]{:S(2)}) collective-permute-start(f32[2,20,128]{2,0,1:T(2,128)} %collective-permute-done.18), channel_id=1, source_target_pairs={{0,16},{8,24},{16,0},{24,8},{1,17},{9,25},{17,1},{25,9},{2,18},{10... | collective-permute-start | bytes 61448 | tf_op jit(solution)/shard_map/ppermute | solution.py:26
  133.1 2.2 %copy-start.16 = (f32[20,32,128]{2,0,1:T(8,128)S(1)}, f32[20,32,128]{2,0,1:T(8,128)}, u32[]{:S(2)}) copy-start(f32[20,32,128]{2,0,1:T(8,128)} %get-tuple-element.15) | copy-start | bytes 983044
  133.1 2.2 %copy-start.17 = (f32[20,32,128]{2,0,1:T(8,128)S(1)}, f32[20,32,128]{2,0,1:T(8,128)}, u32[]{:S(2)}) copy-start(f32[20,32,128]{2,0,1:T(8,128)} %get-tuple-element.16) | copy-start | bytes 983044
  135.5 1.4 copy-start.3
  135.5 1.6 copy-start.4
  137.1 4.8 %copy-start.13 = (f32[2,20,31,128]{3,0,1,2:T(2,128)S(1)}, f32[2,20,31,128]{3,0,1,2:T(2,128)}, u32[]{:S(2)}) copy-start(f32[2,20,31,128]{3,0,1,2:T(2,128)} %get-tuple-element.34) | copy-start | bytes 1904644
  137.1 4.8 %copy-start.15 = (f32[2,19,32,128]{3,0,1,2:T(2,128)S(1)}, f32[2,19,32,128]{3,0,1,2:T(2,128)}, u32[]{:S(2)}) copy-start(f32[2,19,32,128]{3,0,1,2:T(2,128)} %get-tuple-element.47) | copy-start | bytes 1867780
  141.9 2.4 %copy-start.12 = (f32[2,20,31,128]{3,0,1,2:T(2,128)S(1)}, f32[2,20,31,128]{3,0,1,2:T(2,128)}, u32[]{:S(2)}) copy-start(f32[2,20,31,128]{3,0,1,2:T(2,128)} %get-tuple-element.33) | copy-start | bytes 1904644
  141.9 2.4 %copy-start.14 = (f32[2,19,32,128]{3,0,1,2:T(2,128)S(1)}, f32[2,19,32,128]{3,0,1,2:T(2,128)}, u32[]{:S(2)}) copy-start(f32[2,19,32,128]{3,0,1,2:T(2,128)} %get-tuple-element.48) | copy-start | bytes 1867780
  143.3 1.0 copy-start.1
  143.4 1.4 copy-start.8
Sparse Core Ops, SparseCore 0:
  136.6 33.1 reduce-scatter.1
where the time goes:
time: 180 us; the launch traced here: 178 us
  local copies, waits for them, and re-layouts  50.3 us (28%)
  other arithmetic  48 us (27%)
  waiting for transfers between devices  24.5 us (14%)
  starting transfers between devices  23.9 us (13%)
  blocking collectives  17 us (9%)
  between operations  14.5 us (8%)
    reduce_scatter x1, waiting for transfers between devices, on_device(): lax.psum_scatter(summed, 'scen', scatter_dimension=2, tiled=True)  22.6 us
    all_gather x1, blocking collectives, on_device(): full_kappa = lax.all_gather(diffusivity, 'scen', axis=2, tiled=True)  17 us
    slice x9, local copies, waits for them, and re-layouts, with_halo(): lax.slice_in_dim(block, block.shape[dim] - width, None, axis=dim)  12.6 us
    ppermute x10, starting transfers between devices, from_partner(): lax.ppermute(value, axis, [(i, i ^ 1 << stride) for i in range(lax.axis_s...  11.3 us
    mul x2, other arithmetic, operate_on(): east_flux = east_coeff * (edged_field[..., 1:] - edged_field[..., :-1])  10.4 us
    ppermute x5, starting transfers between devices, with_halo(): lax.ppermute(lax.slice_in_dim(block, 0, width, axis=dim), axis, backward)  9.74 us
    reduce_sum x1, other arithmetic, on_device(): jnp.sum(east_mask[..., 1:] * (before_edge[..., 2:] - before_edge[..., 1:-...  8.7 us
    unnamed x53, local copies, waits for them, and re-layouts  8.08 us
  transfers between devices with their start and end apart: 21, of which 3 were waited for; matrix products, arithmetic and copies ran while one was open for 44% of the time, Pallas kernels for 0%

commit v1 on v0

--- a/solution.py
+++ b/solution.py
@@ -6,6 +6,18 @@
 STEPS = 2
 vertical_rate = 0.1
 thaw_rate = 0.3
+
+
+def doubled_up(shard, axis, dim):
+    ways, here, step = (lax.axis_size(axis), lax.axis_index(axis), shard.shape[dim])
+    line, have = (shard, 1)
+    while have < ways:
+        line = jnp.concatenate(
+            [line, lax.ppermute(line, axis, [(d, (d - have) % ways) for d in range(ways)])],
+            axis=dim,
+        )
+        have = 2 * have
+    return jnp.roll(line, here * step, axis=dim)
 
 
 def with_halo(block, sides, width):
@@ -64,7 +76,7 @@
 
 
 def on_device(tracers, diffusivity, level_count, shelf_mask, cotangent):
-    full_kappa = lax.all_gather(diffusivity, "scen", axis=2, tiled=True)
+    full_kappa = doubled_up(diffusivity, "scen", 2)
     levels = lax.broadcasted_iota(jnp.int32, (full_kappa.shape[1],) + level_count.shape, 0)
     wetness = (levels < level_count[None]).astype(jnp.float32)
     sources = sources_of(wetness, shelf_mask)

time: 180 us -> 172 us (0.956)
  blocking collectives: 17 us -> 0 us
  starting transfers between devices: 23.9 us -> 28.9 us
  waiting for transfers between devices: 24.5 us -> 27.7 us
  other arithmetic: 48 us -> 50.3 us
    all_gather x1 -> x0, blocking collectives: 17 us -> none  [on_device(): full_kappa = lax.all_gather(diffusivity, 'scen', axis=2, tiled=True)]
    ppermute x0 -> x3, waiting for transfers between devices: none -> 6.96 us  [doubled_up(): lax.ppermute(line, axis, [(d, (d - have) % ways) for d in range(ways)])]
    concatenate x0 -> x1, local copies, waits for them, and re-layouts: none -> 6.28 us  [doubled_up(): return jnp.roll(line, here * step, axis=dim)]
    ppermute x0 -> x3, starting transfers between devices: none -> 5.26 us  [doubled_up(): lax.ppermute(line, axis, [(d, (d - have) % ways) for d in range(ways)])]
    reduce_scatter x1, waiting for transfers between devices: 22.6 us -> 19.6 us  [on_device(): lax.psum_scatter(summed, 'scen', scatter_dimension=2, tiled=True)]
    unnamed x53 -> x58, local copies, waits for them, and re-layouts: 8.08 us -> 5.12 us
    slice x9, local copies, waits for them, and re-layouts: 12.6 us -> 10.5 us  [with_halo(): lax.slice_in_dim(block, block.shape[dim] - width, None, axis=dim)]
    ppermute x10, waiting for transfers between devices: 1.89 us -> 0.03 us  [from_partner(): lax.ppermute(value, axis, [(i, i ^ 1 << stride) for i in range(lax.axis_s...]
  transfers between devices with their start and end apart: 21 -> 24, of which waited for: 3 -> 4; matrix products, arithmetic and copies ran while one was open for 44% -> 44% of each run, Pallas kernels for 0% -> 0%
where the time goes in v1:
time: 172 us; the launch traced here: 171 us
  other arithmetic  50.3 us (29%)
  local copies, waits for them, and re-layouts  49.7 us (29%)
  starting transfers between devices  28.9 us (17%)
  waiting for transfers between devices  27.7 us (16%)
  between operations  14.6 us (8%)
    reduce_scatter x1, waiting for transfers between devices, on_device(): lax.psum_scatter(summed, 'scen', scatter_dimension=2, tiled=True)  19.6 us
    ppermute x10, starting transfers between devices, from_partner(): lax.ppermute(value, axis, [(i, i ^ 1 << stride) for i in range(lax.axis_s...  10.9 us
    slice x9, local copies, waits for them, and re-layouts, with_halo(): lax.slice_in_dim(block, block.shape[dim] - width, None, axis=dim)  10.5 us
    mul x2, other arithmetic, operate_on(): east_flux = east_coeff * (edged_field[..., 1:] - edged_field[..., :-1])  9.29 us
    ppermute x5, starting transfers between devices, with_halo(): lax.ppermute(lax.slice_in_dim(block, 0, width, axis=dim), axis, backward)  8.75 us
    reduce_sum x1, other arithmetic, on_device(): jnp.sum(east_mask[..., 1:] * (before_edge[..., 2:] - before_edge[..., 1:-...  8.62 us
    ppermute x5, local copies, waits for them, and re-layouts, with_halo(): lax.ppermute(lax.slice_in_dim(block, block.shape[dim] - width, None, axis...  7.24 us
    ppermute x3, waiting for transfers between devices, doubled_up(): lax.ppermute(line, axis, [(d, (d - have) % ways) for d in range(ways)])  6.96 us
  transfers between devices with their start and end apart: 24, of which 4 were waited for; matrix products, arithmetic and copies ran while one was open for 44% of the time, Pallas kernels for 0%

profile of v1, /device:TPU:0, one launch (start us, length us, event | category | flops | bytes accessed | tf_op | source)
XLA Modules:
  0.0 171.1 jit_solution(16213194224031375157)
XLA Ops:
  7.2 4.5 %collective-permute-start = (f32[2,20,4,128]{3,2,1,0:T(4,128)}, f32[2,20,4,128]{3,2,1,0:T(4,128)S(1)}, u32[]{:S(2)}, u32[]{:S(2)}) collective-permute-start(f32[2,20,4,128]{3,2,1,0:T(4,128)} %param.6), channel_id=1, source_target_pairs={{0,7},{1,0},{2,1},{3,2},{4,3},{5,4},{6,5},{7,6},{8,15},{9,8},{10,9... | collective-permute-start | bytes 245768 | tf_op jit(solution)/shard_map/ppermute | solution.py:16
  13.5 1.5 collective-permute-start.17
  17.2 2.5 %collective-permute-start.5 = (f32[2,20,32,1]{2,0,3,1:T(2,128)S(1)}, f32[2,20,32,1]{2,0,3,1:T(2,128)S(1)}, u32[]{:S(2)}, u32[]{:S(2)}) collective-permute-start(f32[2,20,32,1]{2,0,3,1:T(2,128)S(1)} %copy.110), channel_id=1, source_target_pairs={{8,0},{16,8},{24,16},{0,24},{9,1},{17,9},{25,17},{1,25},{10,2},{18... | collective-permute-start | bytes 15368 | tf_op jit(solution)/shard_map/ppermute | solution.py:32
  20.3 1.7 %fusion.38 = (f32[2,19,32,128]{3,0,1,2:T(2,128)}, f32[2,19,32,128]{3,0,1,2:T(2,128)}) fusion(f32[2,20,32,128]{3,0,1,2:T(2,128)S(1)} %bitcast_multiply_fusion, f32[19,32,128]{2,0,1:T(8,128)S(1)} %copy.115, f32[2,20,32,128]{3,0,1,2:T(2,128)S(1)} %bitcast.79), kind=kLoop, calls=%fused_computation.78 | loop fusion | flops 622592 | bytes 4046848 | tf_op jit(solution)/shard_map/mul | solution.py:70
  23.7 4.7 %collective-permute-done.1 = f32[2,20,8,128]{3,2,1,0:T(8,128)S(1)} collective-permute-done((f32[2,20,8,128]{3,2,1,0:T(8,128)S(1)}, f32[2,20,8,128]{3,2,1,0:T(8,128)S(1)}, u32[]{:S(2)}, u32[]{:S(2)}) %collective-permute-start.1) | collective-permute-done | bytes 163872 | tf_op jit(solution)/shard_map/ppermute | solution.py:16
  28.3 0.8 pad_maximum_fusion.6
  29.1 0.8 multiply_bitcast_fusion
  30.6 2.9 %collective-permute-start.15 = (f32[2,20,32,1]{2,0,3,1:T(2,128)S(1)}, f32[2,20,32,1]{2,0,3,1:T(2,128)S(1)}, u32[]{:S(2)}, u32[]{:S(2)}) collective-permute-start(f32[2,20,32,1]{2,0,3,1:T(2,128)S(1)} %copy.122), channel_id=1, source_target_pairs={{8,0},{16,8},{24,16},{0,24},{9,1},{17,9},{25,17},{1,25},{10,2},{18... | collective-permute-start | bytes 15368 | tf_op jit(solution)/shard_map/ppermute | solution.py:32
  34.1 1.5 collective-permute-start.10
  35.6 2.0 %copy.116 = f32[1,20,32,128]{3,0,1,2:T(1,128)} copy(f32[1,20,32,128]{3,2,1,0:T(8,128)} %multiply_bitcast_fusion) | data formatting | bytes 655360 | tf_op jit(solution)/shard_map/stack | solution.py:55
  38.2 1.2 copy.113
  39.3 1.2 copy.123
  40.5 1.2 copy.125
  41.9 2.3 %collective-permute-done.2 = f32[2,20,16,128]{3,2,1,0:T(8,128)} collective-permute-done((f32[2,20,16,128]{3,2,1,0:T(8,128)}, f32[2,20,16,128]{3,2,1,0:T(8,128)}, u32[]{:S(2)}, u32[]{:S(2)}) %collective-permute-start.2) | collective-permute-done | bytes 327712 | tf_op jit(solution)/shard_map/ppermute | solution.py:16
  44.2 6.3 %concatenate.108 = f32[2,20,64,128]{3,2,1,0:T(8,128)} concatenate(f32[2,20,4,128]{3,2,1,0:T(4,128)S(1)} %copy-done.22, f32[2,20,4,128]{3,2,1,0:T(4,128)S(1)} %collective-permute-done, f32[2,20,8,128]{3,2,1,0:T(8,128)S(1)} %collective-permute-done.1, f32[2,20,16,128]{3,2,1,0:T(8,128)} %collective-permute-done.2, f32[2,20,4,128]{3,2,1,0:T(4,128)S(1)} %copy-done.22, ...), dimensions={2} | concatenate | bytes 2621440 | tf_op jit(solution)/shard_map/jit(_roll_dynamic)/concatenate | solution.py:20
  50.5 1.1 dynamic-slice_bitcast_fusion
  51.7 0.8 slice_multiply_fusion.3
  52.5 1.4 collective-permute-start.7
  54.1 1.3 slice_maximum_fusion
  55.4 1.4 copy.105
  56.7 1.4 copy.106
  58.1 1.0 collective-permute-start.4
  59.2 1.0 collective-permute-start.3
  60.2 1.6 subtract_multiply_fusion.1
  61.8 1.0 copy.131
  62.8 1.0 collective-permute-done.3
  63.9 1.2 copy.107
  65.0 1.2 copy.108
  66.2 1.9 %pad_maximum_fusion.4 = f32[2,20,32,130]{3,2,1,0:T(8,128)S(1)} fusion(f32[2,20,32,1]{3,2,1,0:T(8,128)} %copy.108, f32[1,20,32,128]{3,2,1,0:T(8,128)S(1)} %get-tuple-element.23, f32[1,20,32,128]{3,2,1,0:T(8,128)S(1)} %fusion.42, f32[2,20,32,1]{3,2,1,0:T(8,128)} %copy.107), kind=kLoop, calls=%fused_computation.20 | loop fusion | flops 499200 | bytes 1331200 | tf_op jit(solution)/shard_map/concatenate | solution.py:33
  68.9 1.2 collective-permute-start.8
  70.1 4.5 %fusion.3 = (f32[2,20,32,129]{3,0,1,2:T(2,128)}, f32[2,20,32,129]{3,0,1,2:T(2,128)}) fusion(f32[2,20,32,1]{3,0,1,2:T(2,128)S(1)} %copy-done.3, f32[2,20,32,128]{3,0,1,2:T(2,128)S(1)} %bitcast_multiply_fusion, f32[2,20,32,1]{3,0,1,2:T(2,128)S(1)} %copy-done.13, f32[20,32,129]{2,0,1:T(8,128)S(1)} %copy.109, f32[2,20,32,128]{3,0,1,2:T(2,128)S(1)} %bitcast.81, ...), kind=kLoop, calls=%fused_computation.15 | loop fusion | flops 1320960 | bytes 2982400 | tf_op jit(solution)/shard_map/mul | solution.py:61
  74.8 0.9 copy.130
  76.0 0.9 broadcast_multiply_fusion.2
  76.9 6.2 %fusion.33 = (f32[2,20,32,128]{3,0,1,2:T(2,128)S(1)}, f32[2,20,32,128]{3,0,1,2:T(2,128)S(1)}) fusion(f32[2,19,32,128]{3,0,1,2:T(2,128)} %get-tuple-element.48, f32[2,20,31,128]{3,0,1,2:T(2,128)} %get-tuple-element.50, f32[2,20,1,128]{3,0,1,2:T(2,128)S(1)} %get-tuple-element.58, f32[2,20,32,129]{3,0,1,2:T(2,128)} %get-tuple-element.28, ...), kind=kLoop, calls=%fused_computation.65 | loop fusion | flops 2949120 | bytes 8454144 | tf_op jit(solution)/shard_map/mul | solution.py:107
  83.2 1.7 %fusion.44 = (f32[2,20,32,1]{3,0,1,2:T(2,128)}, f32[2,20,32,1]{3,0,1,2:T(2,128)}) fusion(f32[2,20,32,128]{3,0,1,2:T(2,128)S(1)} %get-tuple-element.46), kind=kLoop, calls=%fused_computation.118 | loop fusion | bytes 20480 | tf_op jit(solution)/shard_map/slice | solution.py:30
  84.9 1.8 %fusion.46 = (f32[2,20,32,1]{3,0,1,2:T(2,128)}, f32[2,20,32,1]{3,0,1,2:T(2,128)}) fusion(f32[2,20,32,128]{3,0,1,2:T(2,128)S(1)} %get-tuple-element.47), kind=kLoop, calls=%fused_computation.120 | loop fusion | bytes 20480 | tf_op jit(solution)/shard_map/slice | solution.py:30
  87.2 1.5 collective-permute-start.21
  88.7 6.7 %multiply_reduce_fusion = (f32[20,31,128]{2,0,1:T(8,128)}, f32[20,31,128]{2,0,1:T(8,128)}, f32[2,20,31,128]{3,0,1,2:T(2,128)}, f32[2,20,31,128]{3,0,1,2:T(2,128)}) fusion(f32[2,20,32,128]{3,0,1,2:T(2,128)S(1)} %get-tuple-element.46, f32[20,31,128]{2,0,1:T(8,128)S(1)} %copy-done.20, f32[2,20,32,128]{3,0,1,2:T(2,128)S(1)} %bitcast.83, ...), kind=kLoop, calls=%fused_computation.71 | loop fusion | flops 1904640 | bytes 7618560 | tf_op jit(solution)/shard_map/reduce_sum | solution.py:117
  95.4 2.0 %copy.126 = f32[2,20,32,1]{2,0,3,1:T(2,128)} copy(f32[2,20,32,1]{3,0,1,2:T(2,128)} %get-tuple-element.35) | data formatting | bytes 10240 | tf_op jit(solution)/shard_map/slice | solution.py:32
  97.4 0.8 collective-permute-start.19
  98.2 2.0 %copy.117 = f32[2,20,32,1]{2,0,3,1:T(2,128)} copy(f32[2,20,32,1]{3,0,1,2:T(2,128)} %get-tuple-element.39) | data formatting | bytes 10240 | tf_op jit(solution)/shard_map/slice | solution.py:32
  100.2 1.5 collective-permute-start.11
  101.7 2.7 %fusion.37 = (f32[2,19,32,128]{3,0,1,2:T(2,128)}, f32[2,19,32,128]{3,0,1,2:T(2,128)}) fusion(f32[2,20,32,128]{3,0,1,2:T(2,128)S(1)} %get-tuple-element.46, f32[19,32,128]{2,0,1:T(8,128)} %copy-done.6, f32[2,20,32,128]{3,0,1,2:T(2,128)S(1)} %get-tuple-element.47), kind=kLoop, calls=%fused_computation.76 | loop fusion | flops 622592 | bytes 4046848 | tf_op jit(solution)/shard_map/mul | solution.py:70
  104.4 1.4 copy.128
  105.8 0.8 collective-permute-start.20
  106.6 2.0 %copy.119 = f32[2,20,32,1]{2,0,3,1:T(2,128)} copy(f32[2,20,32,1]{3,0,1,2:T(2,128)} %get-tuple-element.38) | data formatting | bytes 10240 | tf_op jit(solution)/shard_map/slice | solution.py:30
  108.6 2.1 %collective-permute-start.12 = (f32[2,20,32,1]{2,0,3,1:T(2,128)}, f32[2,20,32,1]{2,0,3,1:T(2,128)}, u32[]{:S(2)}, u32[]{:S(2)}) collective-permute-start(f32[2,20,32,1]{2,0,3,1:T(2,128)} %copy.119), channel_id=1, source_target_pairs={{0,8},{8,16},{16,24},{24,0},{1,9},{9,17},{17,25},{25,1},{2,10},{10... | collective-permute-start | bytes 15368 | tf_op jit(solution)/shard_map/ppermute | solution.py:29
  110.7 1.9 %copy.127 = f32[2,20,32,1]{3,0,1,2:T(2,128)} copy(f32[2,20,32,1]{2,0,3,1:T(2,128)} %collective-permute-done.19) | data formatting | bytes 10240 | tf_op jit(solution)/shard_map/ppermute | solution.py:32
  112.6 1.9 %copy.118 = f32[2,20,32,1]{3,0,1,2:T(2,128)} copy(f32[2,20,32,1]{2,0,3,1:T(2,128)} %collective-permute-done.11) | data formatting | bytes 10240 | tf_op jit(solution)/shard_map/ppermute | solution.py:32
  114.4 0.9 collective-permute-start.14
  115.3 1.2 collective-permute-start.22
  116.5 8.6 %fusion.36 = (f32[20,32,128]{2,0,1:T(8,128)}, f32[20,32,128]{2,0,1:T(8,128)}) fusion(f32[2,20,32,128]{3,0,1,2:T(2,128)S(1)} %get-tuple-element.46, f32[2,20,32,1]{3,0,1,2:T(2,128)} %copy.127, f32[2,20,32,128]{3,0,1,2:T(2,128)S(1)} %bitcast.84, f32[2,20,32,1]{3,0,1,2:T(2,128)} %copy-done.2, f32[20,32,128]{2,0,1:T(8,128)} %copy.130, ...), kind=kLoop, calls=%fused_computation.68 | loop fusion | flops 2129920 | bytes 3624960 | tf_op jit(solution)/shard_map/reduce_sum | solution.py:111
  125.1 1.9 %copy.129 = f32[2,20,32,1]{3,0,1,2:T(2,128)} copy(f32[2,20,32,1]{2,0,3,1:T(2,128)} %collective-permute-done.20) | data formatting | bytes 10240 | tf_op jit(solution)/shard_map/ppermute | solution.py:29
  127.0 1.9 %copy.120 = f32[2,20,32,1]{3,0,1,2:T(2,128)} copy(f32[2,20,32,1]{2,0,3,1:T(2,128)} %collective-permute-done.12) | data formatting | bytes 10240 | tf_op jit(solution)/shard_map/ppermute | solution.py:29
  129.2 1.1 maximum_bitcast_fusion.1
  130.3 1.0 maximum_bitcast_fusion
  131.5 0.9 copy.132
  133.0 4.8 %fusion.1 = (f32[2,20,32,129]{3,0,1,2:T(2,128)S(1)}, f32[2,20,32,129]{3,0,1,2:T(2,128)S(1)}) fusion(f32[2,20,32,1]{3,0,1,2:T(2,128)S(1)} %copy-done.4, f32[2,20,32,128]{3,0,1,2:T(2,128)S(1)} %get-tuple-element.46, f32[2,20,32,1]{3,0,1,2:T(2,128)} %copy.129, f32[20,32,129]{2,0,1:T(8,128)S(1)} %copy.109, f32[2,20,32,128]{3,0,1,2:T(2,128)S(1)} %get-tuple-element.47, ...), kind=kLoop, calls=%fused_computation.13 | loop fusion | flops 1320960 | bytes 2982400 | tf_op jit(solution)/shard_map/mul | solution.py:61
  137.9 1.4 fusion.34
  139.3 1.0 copy.134
  140.6 1.6 fusion.10
  142.2 1.0 copy.133
  143.1 19.6 %reduce-scatter.2.cloned.1.call-done = f32[2,20,4,128]{3,1,0,2:T(8,128)} async-done(((f32[2,20,32,128]{3,1,0,2:T(8,128)}), f32[2,20,4,128]{3,1,0,2:T(8,128)}) %reduce-scatter.2.cloned.1.call-update) | async-done | bytes 81936 | tf_op jit(solution)/shard_map/reduce_scatter | solution.py:134
  162.7 1.6 copy.135
  (120 shorter events, 11.5 us)
Async XLA Ops:
  7.2 5.6 %copy-start.10 = (f32[1,2,20,32,128]{4,3,2,1,0:T(8,128)S(1)}, f32[1,2,20,32,128]{4,3,2,1,0:T(8,128)}, u32[]{:S(2)}) copy-start(f32[1,2,20,32,128]{4,3,2,1,0:T(8,128)} %param.9) | copy-start | bytes 1966084
  7.2 155.6 %reduce-scatter.2.cloned.1.call-start = ((), (), s32[]{:S(2)}) async-start(), calls=%async_computation.1 | async-start | bytes 884736 | tf_op jit(solution)/shard_map/reduce_scatter | solution.py:134
  7.2 15.6 %collective-permute-start = (f32[2,20,4,128]{3,2,1,0:T(4,128)}, f32[2,20,4,128]{3,2,1,0:T(4,128)S(1)}, u32[]{:S(2)}, u32[]{:S(2)}) collective-permute-start(f32[2,20,4,128]{3,2,1,0:T(4,128)} %param.6), channel_id=1, source_target_pairs={{0,7},{1,0},{2,1},{3,2},{4,3},{5,4},{6,5},{7,6},{8,15},{9,8},{10,9... | collective-permute-start | bytes 245768 | tf_op jit(solution)/shard_map/ppermute | solution.py:16
  12.5 2.5 %copy-start.11 = (f32[1,2,20,32,128]{4,3,2,1,0:T(8,128)S(1)}, f32[1,2,20,32,128]{4,3,2,1,0:T(8,128)}, u32[]{:S(2)}) copy-start(f32[1,2,20,32,128]{4,3,2,1,0:T(8,128)} %param.5) | copy-start | bytes 1966084
  12.7 0.8 copy-start
  13.5 20.0 %collective-permute-start.17 = (f32[2,20,128]{2,0,1:T(2,128)S(1)}, f32[2,20,128]{2,0,1:T(2,128)S(1)}, u32[]{:S(2)}, u32[]{:S(2)}) collective-permute-start(f32[2,20,128]{2,0,1:T(2,128)S(1)} %slice_bitcast_fusion.3), channel_id=1, source_target_pairs={{0,8},{8,0},{16,24},{24,16},{1,9},{9,1},{17,25},{25,17},{2,10},{10... | collective-permute-start | bytes 61448 | tf_op jit(solution)/shard_map/ppermute | solution.py:38
  15.5 18.6 %collective-permute-start.9 = (f32[2,20,128]{2,0,1:T(2,128)S(1)}, f32[2,20,128]{2,0,1:T(2,128)S(1)}, u32[]{:S(2)}, u32[]{:S(2)}) collective-permute-start(f32[2,20,128]{2,0,1:T(2,128)S(1)} %slice_bitcast_fusion.5), channel_id=1, source_target_pairs={{0,8},{8,0},{16,24},{24,16},{1,9},{9,1},{17,25},{25,17},{2,10},{10... | collective-permute-start | bytes 61448 | tf_op jit(solution)/shard_map/ppermute | solution.py:38
  17.2 13.4 %collective-permute-start.5 = (f32[2,20,32,1]{2,0,3,1:T(2,128)S(1)}, f32[2,20,32,1]{2,0,3,1:T(2,128)S(1)}, u32[]{:S(2)}, u32[]{:S(2)}) collective-permute-start(f32[2,20,32,1]{2,0,3,1:T(2,128)S(1)} %copy.110), channel_id=1, source_target_pairs={{8,0},{16,8},{24,16},{0,24},{9,1},{17,9},{25,17},{1,25},{10,2},{18... | collective-permute-start | bytes 15368 | tf_op jit(solution)/shard_map/ppermute | solution.py:32
  20.0 13.5 %collective-permute-start.6 = (f32[2,20,32,1]{2,0,3,1:T(2,128)S(1)}, f32[2,20,32,1]{2,0,3,1:T(2,128)S(1)}, u32[]{:S(2)}, u32[]{:S(2)}) collective-permute-start(f32[2,20,32,1]{2,0,3,1:T(2,128)S(1)} %copy.112), channel_id=1, source_target_pairs={{0,8},{8,16},{16,24},{24,0},{1,9},{9,17},{17,25},{25,1},{2,10},{10... | collective-permute-start | bytes 15368 | tf_op jit(solution)/shard_map/ppermute | solution.py:29
  20.3 1.7 %copy-start.6 = (f32[19,32,128]{2,0,1:T(8,128)}, f32[19,32,128]{2,0,1:T(8,128)S(1)}, u32[]{:S(2)}) copy-start(f32[19,32,128]{2,0,1:T(8,128)S(1)} %copy.115) | copy-start | bytes 933892
  22.0 0.9 copy-start.22
  22.0 1.6 copy-start.25
  22.0 7.1 %copy-start.24 = (s32[32,128]{1,0:T(8,128)S(1)}, s32[32,128]{1,0:T(8,128)}, u32[]{:S(2)}) copy-start(s32[32,128]{1,0:T(8,128)} %param.7) | copy-start | bytes 49156
  23.0 5.4 %collective-permute-start.1 = (f32[2,20,8,128]{3,2,1,0:T(8,128)S(1)}, f32[2,20,8,128]{3,2,1,0:T(8,128)S(1)}, u32[]{:S(2)}, u32[]{:S(2)}) collective-permute-start(f32[2,20,8,128]{3,2,1,0:T(8,128)S(1)} %pad_maximum_fusion.7), channel_id=1, source_target_pairs={{0,6},{1,7},{2,0},{3,1},{4,2},{5,3},{6,4},{7,5},{8,14},{9,15},{10,... | collective-permute-start | bytes 491528 | tf_op jit(solution)/shard_map/ppermute | solution.py:16
  29.1 15.1 %collective-permute-start.2 = (f32[2,20,16,128]{3,2,1,0:T(8,128)}, f32[2,20,16,128]{3,2,1,0:T(8,128)}, u32[]{:S(2)}, u32[]{:S(2)}) collective-permute-start(f32[2,20,16,128]{3,2,1,0:T(8,128)} %pad_maximum_fusion.6), channel_id=1, source_target_pairs={{0,4},{1,5},{2,6},{3,7},{4,0},{5,1},{6,2},{7,3},{8,12},{9,13},{10,... | collective-permute-start | bytes 983048 | tf_op jit(solution)/shard_map/ppermute | solution.py:16
  30.6 8.8 %collective-permute-start.15 = (f32[2,20,32,1]{2,0,3,1:T(2,128)S(1)}, f32[2,20,32,1]{2,0,3,1:T(2,128)S(1)}, u32[]{:S(2)}, u32[]{:S(2)}) collective-permute-start(f32[2,20,32,1]{2,0,3,1:T(2,128)S(1)} %copy.122), channel_id=1, source_target_pairs={{8,0},{16,8},{24,16},{0,24},{9,1},{17,9},{25,17},{1,25},{10,2},{18... | collective-permute-start | bytes 15368 | tf_op jit(solution)/shard_map/ppermute | solution.py:32
  33.5 7.0 %collective-permute-start.16 = (f32[2,20,32,1]{2,0,3,1:T(2,128)S(1)}, f32[2,20,32,1]{2,0,3,1:T(2,128)S(1)}, u32[]{:S(2)}, u32[]{:S(2)}) collective-permute-start(f32[2,20,32,1]{2,0,3,1:T(2,128)S(1)} %copy.124), channel_id=1, source_target_pairs={{0,8},{8,16},{16,24},{24,0},{1,9},{9,17},{17,25},{25,1},{2,10},{10... | collective-permute-start | bytes 15368 | tf_op jit(solution)/shard_map/ppermute | solution.py:29
  33.5 8.2 %collective-permute-start.18 = (f32[2,20,128]{2,0,1:T(2,128)S(1)}, f32[2,20,128]{2,0,1:T(2,128)S(1)}, u32[]{:S(2)}, u32[]{:S(2)}) collective-permute-start(f32[2,20,128]{2,0,1:T(2,128)S(1)} %collective-permute-done.17), channel_id=1, source_target_pairs={{0,16},{8,24},{16,0},{24,8},{1,17},{9,25},{17,1},{25,9},{2,18},{10... | collective-permute-start | bytes 61448 | tf_op jit(solution)/shard_map/ppermute | solution.py:38
  34.1 7.6 %collective-permute-start.10 = (f32[2,20,128]{2,0,1:T(2,128)S(1)}, f32[2,20,128]{2,0,1:T(2,128)S(1)}, u32[]{:S(2)}, u32[]{:S(2)}) collective-permute-start(f32[2,20,128]{2,0,1:T(2,128)S(1)} %collective-permute-done.9), channel_id=1, source_target_pairs={{0,16},{8,24},{16,0},{24,8},{1,17},{9,25},{17,1},{25,9},{2,18},{10... | collective-permute-start | bytes 61448 | tf_op jit(solution)/shard_map/ppermute | solution.py:38
  38.2 32.0 %copy-start.2 = (f32[2,20,32,1]{3,0,1,2:T(2,128)}, f32[2,20,32,1]{3,0,1,2:T(2,128)S(1)}, u32[]{:S(2)}) copy-start(f32[2,20,32,1]{3,0,1,2:T(2,128)S(1)} %copy.111) | copy-start | bytes 15364
  51.6 2.3 %copy-start.21 = (f32[20,32,128]{2,1,0:T(8,128)}, f32[20,32,128]{2,1,0:T(8,128)S(1)}, u32[]{:S(2)}) copy-start(f32[20,32,128]{2,1,0:T(8,128)S(1)} %get-tuple-element.22) | copy-start | bytes 983044
  52.5 16.4 %collective-permute-start.7 = (f32[2,20,128]{2,0,1:T(2,128)S(1)}, f32[2,20,128]{2,0,1:T(2,128)S(1)}, u32[]{:S(2)}, u32[]{:S(2)}) collective-permute-start(f32[2,20,128]{2,0,1:T(2,128)S(1)} %pad_maximum_fusion.8), channel_id=1, source_target_pairs={{0,8},{8,0},{16,24},{24,16},{1,9},{9,1},{17,25},{25,17},{2,10},{10... | collective-permute-start | bytes 61448 | tf_op jit(solution)/shard_map/ppermute | solution.py:38
  54.1 6.1 %copy-start.7 = (f32[20,31,128]{2,0,1:T(8,128)}, f32[20,31,128]{2,0,1:T(8,128)S(1)}, u32[]{:S(2)}) copy-start(f32[20,31,128]{2,0,1:T(8,128)S(1)} %copy.114) | copy-start | bytes 952324
  58.1 3.7 %copy-start.23 = (f32[20,31,128]{2,1,0:T(8,128)S(1)}, f32[20,31,128]{2,1,0:T(8,128)}, u32[]{:S(2)}) copy-start(f32[20,31,128]{2,1,0:T(8,128)} %get-tuple-element.19) | copy-start | bytes 952324
  58.1 6.9 %collective-permute-start.4 = (f32[2,20,32,1]{2,0,3,1:T(2,128)S(1)}, f32[2,20,32,1]{2,0,3,1:T(2,128)S(1)}, u32[]{:S(2)}, u32[]{:S(2)}) collective-permute-start(f32[2,20,32,1]{2,0,3,1:T(2,128)S(1)} %copy.106), channel_id=1, source_target_pairs={{8,0},{16,8},{24,16},{0,24},{9,1},{17,9},{25,17},{1,25},{10,2},{18... | collective-permute-start | bytes 15368 | tf_op jit(solution)/shard_map/ppermute | solution.py:32
  59.2 4.7 %collective-permute-start.3 = (f32[2,20,32,1]{2,0,3,1:T(2,128)S(1)}, f32[2,20,32,1]{2,0,3,1:T(2,128)S(1)}, u32[]{:S(2)}, u32[]{:S(2)}) collective-permute-start(f32[2,20,32,1]{2,0,3,1:T(2,128)S(1)} %copy.105), channel_id=1, source_target_pairs={{0,8},{8,16},{16,24},{24,0},{1,9},{9,17},{17,25},{25,1},{2,10},{10... | collective-permute-start | bytes 15368 | tf_op jit(solution)/shard_map/ppermute | solution.py:29
  68.2 1.9 %copy-start.13 = (f32[2,20,32,1]{3,0,1,2:T(2,128)S(1)}, f32[2,20,32,1]{3,0,1,2:T(2,128)}, u32[]{:S(2)}) copy-start(f32[2,20,32,1]{3,0,1,2:T(2,128)} %copy.125) | copy-start | bytes 15364
  68.5 1.7 copy-start.3
  68.5 1.7 copy-start.12
  68.9 6.8 %collective-permute-start.8 = (f32[2,20,128]{2,0,1:T(2,128)S(1)}, f32[2,20,128]{2,0,1:T(2,128)S(1)}, u32[]{:S(2)}, u32[]{:S(2)}) collective-permute-start(f32[2,20,128]{2,0,1:T(2,128)S(1)} %collective-permute-done.7), channel_id=1, source_target_pairs={{0,16},{8,24},{16,0},{24,8},{1,17},{9,25},{17,1},{25,9},{2,18},{10... | collective-permute-start | bytes 61448 | tf_op jit(solution)/shard_map/ppermute | solution.py:38
  84.9 3.8 %copy-start.8 = (f32[20,31,128]{2,0,1:T(8,128)S(1)}, f32[20,31,128]{2,0,1:T(8,128)}, u32[]{:S(2)}) copy-start(f32[20,31,128]{2,0,1:T(8,128)} %copy-done.7) | copy-start | bytes 952324
  84.9 3.8 %copy-start.20 = (f32[20,31,128]{2,0,1:T(8,128)S(1)}, f32[20,31,128]{2,0,1:T(8,128)}, u32[]{:S(2)}) copy-start(f32[20,31,128]{2,0,1:T(8,128)} %copy.131) | copy-start | bytes 952324
  86.7 27.7 %collective-permute-start.13 = (f32[2,20,128]{2,0,1:T(2,128)S(1)}, f32[2,20,128]{2,0,1:T(2,128)}, u32[]{:S(2)}, u32[]{:S(2)}) collective-permute-start(f32[2,20,128]{2,0,1:T(2,128)S(1)} %slice_bitcast_fusion.4), channel_id=1, source_target_pairs={{0,8},{8,0},{16,24},{24,16},{1,9},{9,1},{17,25},{25,17},{2,10},{10... | collective-permute-start | bytes 61448 | tf_op jit(solution)/shard_map/ppermute | solution.py:38
  87.2 28.1 %collective-permute-start.21 = (f32[2,20,128]{2,0,1:T(2,128)S(1)}, f32[2,20,128]{2,0,1:T(2,128)}, u32[]{:S(2)}, u32[]{:S(2)}) collective-permute-start(f32[2,20,128]{2,0,1:T(2,128)S(1)} %slice_bitcast_fusion.2), channel_id=1, source_target_pairs={{0,8},{8,0},{16,24},{24,16},{1,9},{9,1},{17,25},{25,17},{2,10},{10... | collective-permute-start | bytes 61448 | tf_op jit(solution)/shard_map/ppermute | solution.py:38
  97.4 11.2 %collective-permute-start.19 = (f32[2,20,32,1]{2,0,3,1:T(2,128)}, f32[2,20,32,1]{2,0,3,1:T(2,128)}, u32[]{:S(2)}, u32[]{:S(2)}) collective-permute-start(f32[2,20,32,1]{2,0,3,1:T(2,128)} %copy.126), channel_id=1, source_target_pairs={{8,0},{16,8},{24,16},{0,24},{9,1},{17,9},{25,17},{1,25},{10,2},{18... | collective-permute-start | bytes 15368 | tf_op jit(solution)/shard_map/ppermute | solution.py:32
  100.2 12.3 %collective-permute-start.11 = (f32[2,20,32,1]{2,0,3,1:T(2,128)}, f32[2,20,32,1]{2,0,3,1:T(2,128)}, u32[]{:S(2)}, u32[]{:S(2)}) collective-permute-start(f32[2,20,32,1]{2,0,3,1:T(2,128)} %copy.117), channel_id=1, source_target_pairs={{8,0},{16,8},{24,16},{0,24},{9,1},{17,9},{25,17},{1,25},{10,2},{18... | collective-permute-start | bytes 15368 | tf_op jit(solution)/shard_map/ppermute | solution.py:32
  105.8 19.3 %collective-permute-start.20 = (f32[2,20,32,1]{2,0,3,1:T(2,128)S(1)}, f32[2,20,32,1]{2,0,3,1:T(2,128)}, u32[]{:S(2)}, u32[]{:S(2)}) collective-permute-start(f32[2,20,32,1]{2,0,3,1:T(2,128)S(1)} %copy.128), channel_id=1, source_target_pairs={{0,8},{8,16},{16,24},{24,0},{1,9},{9,17},{17,25},{25,1},{2,10},{10... | collective-permute-start | bytes 15368 | tf_op jit(solution)/shard_map/ppermute | solution.py:29
  108.6 18.4 %collective-permute-start.12 = (f32[2,20,32,1]{2,0,3,1:T(2,128)}, f32[2,20,32,1]{2,0,3,1:T(2,128)}, u32[]{:S(2)}, u32[]{:S(2)}) collective-permute-start(f32[2,20,32,1]{2,0,3,1:T(2,128)} %copy.119), channel_id=1, source_target_pairs={{0,8},{8,16},{16,24},{24,0},{1,9},{9,17},{17,25},{25,1},{2,10},{10... | collective-permute-start | bytes 15368 | tf_op jit(solution)/shard_map/ppermute | solution.py:29
  114.4 14.4 %collective-permute-start.14 = (f32[2,20,128]{2,0,1:T(2,128)}, f32[2,20,128]{2,0,1:T(2,128)S(1)}, u32[]{:S(2)}, u32[]{:S(2)}) collective-permute-start(f32[2,20,128]{2,0,1:T(2,128)} %collective-permute-done.13), channel_id=1, source_target_pairs={{0,16},{8,24},{16,0},{24,8},{1,17},{9,25},{17,1},{25,9},{2,18},{10... | collective-permute-start | bytes 61448 | tf_op jit(solution)/shard_map/ppermute | solution.py:38
  115.3 13.7 %collective-permute-start.22 = (f32[2,20,128]{2,0,1:T(2,128)}, f32[2,20,128]{2,0,1:T(2,128)S(1)}, u32[]{:S(2)}, u32[]{:S(2)}) collective-permute-start(f32[2,20,128]{2,0,1:T(2,128)} %collective-permute-done.21), channel_id=1, source_target_pairs={{0,16},{8,24},{16,0},{24,8},{1,17},{9,25},{17,1},{25,9},{2,18},{10... | collective-permute-start | bytes 61448 | tf_op jit(solution)/shard_map/ppermute | solution.py:38
  129.1 2.2 %copy-start.18 = (f32[20,32,128]{2,0,1:T(8,128)S(1)}, f32[20,32,128]{2,0,1:T(8,128)}, u32[]{:S(2)}) copy-start(f32[20,32,128]{2,0,1:T(8,128)} %get-tuple-element.12) | copy-start | bytes 983044
  129.1 2.2 %copy-start.19 = (f32[20,32,128]{2,0,1:T(8,128)S(1)}, f32[20,32,128]{2,0,1:T(8,128)}, u32[]{:S(2)}) copy-start(f32[20,32,128]{2,0,1:T(8,128)} %get-tuple-element.13) | copy-start | bytes 983044
  131.5 1.4 copy-start.4
  131.5 1.6 copy-start.5
  133.0 4.8 %copy-start.15 = (f32[2,20,31,128]{3,0,1,2:T(2,128)S(1)}, f32[2,20,31,128]{3,0,1,2:T(2,128)}, u32[]{:S(2)}) copy-start(f32[2,20,31,128]{3,0,1,2:T(2,128)} %get-tuple-element.33) | copy-start | bytes 1904644
  133.0 4.8 %copy-start.17 = (f32[2,19,32,128]{3,0,1,2:T(2,128)S(1)}, f32[2,19,32,128]{3,0,1,2:T(2,128)}, u32[]{:S(2)}) copy-start(f32[2,19,32,128]{3,0,1,2:T(2,128)} %get-tuple-element.44) | copy-start | bytes 1867780
  137.9 2.4 %copy-start.14 = (f32[2,20,31,128]{3,0,1,2:T(2,128)S(1)}, f32[2,20,31,128]{3,0,1,2:T(2,128)}, u32[]{:S(2)}) copy-start(f32[2,20,31,128]{3,0,1,2:T(2,128)} %get-tuple-element.32) | copy-start | bytes 1904644
  137.9 2.4 %copy-start.16 = (f32[2,19,32,128]{3,0,1,2:T(2,128)S(1)}, f32[2,19,32,128]{3,0,1,2:T(2,128)}, u32[]{:S(2)}) copy-start(f32[2,19,32,128]{3,0,1,2:T(2,128)} %get-tuple-element.45) | copy-start | bytes 1867780
  139.3 1.0 copy-start.1
  139.3 1.2 copy-start.9
Sparse Core Ops, SparseCore 0:
  132.6 30.1 reduce-scatter.1
